TPU v7x, 512 devices: a whole 4x8x8 slice. The times are simulated.
512 devices in a mesh: patch: 128 (over y, z_lo, x), chan: 4 (over z_hi, core).
Axes of the slice: x: 4, y: 8, z: 8 (z_hi: 2, z_lo: 4; z = z_hi * 4 + z_lo), core: 2. Of those that a mesh axis runs over, the one named last changes fastest.
Arguments:
- latent: bfloat16 [8192, 1280], P('patch', 'chan'), may hold values from -6 to 6
- timestep: int32 [1], replicated, may hold values from 0 to 999
- norm_gain: float32 [1280], P('chan'), may hold values from 0.25 to 1.75
- norm_bias: float32 [1280], P('chan'), may hold values from -3 to 3
- w_time: bfloat16 [320, 1280], P(None, 'chan'), may hold values from -0.3125 to 0.3125
- w_query: bfloat16 [1280, 1024], P(None, 'chan'), may hold values from -0.15625 to 0.15625
- w_key: bfloat16 [1280, 1024], P(None, 'chan'), may hold values from -0.3125 to 0.3125
- w_value: bfloat16 [1280, 1024], P(None, 'chan'), may hold values from -0.15625 to 0.15625
- w_out: bfloat16 [1024, 1280], P('chan'), may hold values from -0.1875 to 0.1875
- stale_keys: bfloat16 [8192, 1024], P('patch', 'chan'), may hold values from -12 to 12
- stale_values: bfloat16 [8192, 1024], P('patch', 'chan'), may hold values from -6 to 6
Outputs:
- mixed: bfloat16 [8192, 1280], P('patch', 'chan')
- fresh_keys: bfloat16 [8192, 1024], P('patch', 'chan')
- fresh_values: bfloat16 [8192, 1024], P('patch', 'chan')
All inputs are finite; a program needn't handle non-finite values.
Results may differ from a plain program's by a relative error of at most 0.006.
Values may be sent and summed in bfloat16 or wider, within the bound.
No kernel may reach another device: no remote copies, remote signals or barrier semaphores. Data moves between devices by JAX's collectives and lax.ppermute only.
A program may use at most 64 MiB of HBM per device.

v0:
```python
import math
import jax
import jax.numpy as jnp
from jax import lax
from jax.sharding import PartitionSpec as P

D = 1280
HEAD_DIM = 64
GROUPS = 32


def timestep_shift(timestep, w_time):
    half_dim = w_time.shape[0] // 2
    frequency = jnp.exp(-math.log(10000.0) * jnp.arange(half_dim, dtype=jnp.float32) / half_dim)
    angles = timestep[0].astype(jnp.float32) * frequency
    embedding = jnp.concatenate([jnp.cos(angles), jnp.sin(angles)])
    return jnp.dot(
        jax.nn.silu(embedding)[None, :], w_time.astype(jnp.float32), precision=lax.Precision.HIGHEST
    )[0]


def local(
    latent,
    timestep,
    norm_gain,
    norm_bias,
    w_time,
    w_query,
    w_key,
    w_value,
    w_out,
    stale_keys,
    stale_values,
):
    rows_here, chan_width = latent.shape
    patch_count = lax.axis_size("patch")
    chan_count = lax.axis_size("chan")
    device = lax.axis_index("patch")
    local_groups = GROUPS // chan_count
    width = D // GROUPS
    values = latent.astype(jnp.float32).reshape(rows_here, local_groups, width)
    amount = rows_here * patch_count * width
    group_total = lax.psum(jnp.sum(values, axis=(0, 2)), "patch")
    group_mean = group_total / amount
    centered = values - group_mean[None, :, None]
    spread = lax.psum(jnp.sum(centered * centered, axis=(0, 2)), "patch")
    variance = spread / amount
    scaled = (centered * lax.rsqrt(variance + 1e-05)[None, :, None]).reshape(rows_here, chan_width)
    normed = (scaled * norm_gain + norm_bias + timestep_shift(timestep, w_time)).astype(
        jnp.bfloat16
    )
    inner = w_query.shape[1]
    shard_piece = lax.all_gather(normed, "chan", axis=1, tiled=True)
    outputs = []
    for index, weight_matrix in enumerate((w_query, w_key, w_value)):
        outputs.append(jnp.dot(shard_piece, weight_matrix, preferred_element_type=jnp.float32))
    summed = tuple(outputs)
    queries = summed[0].astype(jnp.bfloat16)
    fresh_keys = summed[1].astype(jnp.bfloat16)
    fresh_values = summed[2].astype(jnp.bfloat16)
    heads_here = inner // HEAD_DIM
    score_scale = HEAD_DIM ** (-0.5)
    query_heads = queries.reshape(rows_here, heads_here, HEAD_DIM)

    def slab_stats(key_block, value_block):
        score = (
            jnp.einsum("qhd,skhd->hqsk", query_heads, key_block, preferred_element_type=jnp.float32)
            * score_scale
        )
        block_max = jnp.max(score, axis=-1)
        weight = jnp.exp(score - block_max[..., None]).astype(jnp.bfloat16)
        block_num = jnp.einsum(
            "hqsk,skhd->hqsd", weight, value_block, preferred_element_type=jnp.float32
        )
        block_den = jnp.sum(weight.astype(jnp.float32), axis=-1)
        return (block_max, block_num, block_den)

    def combine(running, block_max, block_num, block_den):
        run_max, run_num, run_den = running
        new_max = jnp.maximum(run_max, jnp.max(block_max, axis=-1))
        keep_old = jnp.exp(run_max - new_max)
        factor = jnp.exp(block_max - new_max[..., None])
        run_num = keep_old[..., None] * run_num + jnp.sum(factor[..., None] * block_num, axis=2)
        run_den = keep_old * run_den + jnp.sum(factor * block_den, axis=2)
        return (new_max, run_num, run_den)

    home_max, home_num, home_den = slab_stats(
        fresh_keys.reshape(1, rows_here, heads_here, HEAD_DIM),
        fresh_values.reshape(1, rows_here, heads_here, HEAD_DIM),
    )
    start_state = (home_max[..., 0], home_num[:, :, 0], home_den[..., 0])
    key_piece = lax.all_gather(stale_keys, "patch", axis=0, tiled=True)
    value_piece = lax.all_gather(stale_values, "patch", axis=0, tiled=True)
    slab_count = key_piece.shape[0] // rows_here
    per_step = math.gcd(slab_count, 8)
    key_steps = key_piece.reshape(slab_count // per_step, per_step, rows_here, heads_here, HEAD_DIM)
    value_steps = value_piece.reshape(
        slab_count // per_step, per_step, rows_here, heads_here, HEAD_DIM
    )

    def advance(state, inputs):
        key_block, value_block, index = inputs
        block_max, block_num, block_den = slab_stats(key_block, value_block)
        slab_ids = index * per_step + jnp.arange(per_step, dtype=jnp.int32)
        is_home = slab_ids == device
        block_max = jnp.where(is_home[None, None, :], -1e30, block_max)
        return (combine(state, block_max, block_num, block_den), None)

    step_ids = jnp.arange(slab_count // per_step, dtype=jnp.int32)
    result, unused = lax.scan(advance, start_state, (key_steps, value_steps, step_ids))
    final_max, final_num, final_den = result
    attended = (
        jnp.transpose(final_num / final_den[..., None], (1, 0, 2))
        .reshape(rows_here, inner)
        .astype(jnp.bfloat16)
    )
    projected = lax.psum_scatter(
        jnp.dot(attended, w_out, preferred_element_type=jnp.float32).T,
        "chan",
        scatter_dimension=0,
        tiled=True,
    ).T
    mixed = (latent.astype(jnp.float32) + projected).astype(jnp.bfloat16)
    return (mixed, fresh_keys, fresh_values)


def solution(mesh):
    in_specs = (
        P("patch", "chan"),
        P(),
        P("chan"),
        P("chan"),
        P(None, "chan"),
        P(None, "chan"),
        P(None, "chan"),
        P(None, "chan"),
        P("chan", None),
        P("patch", "chan"),
        P("patch", "chan"),
    )
    out_specs = (P("patch", "chan"), P("patch", "chan"), P("patch", "chan"))
    return jax.shard_map(local, mesh=mesh, in_specs=in_specs, out_specs=out_specs, check_vma=False)
```

profile of v0, /device:TPU:1, one launch (start us, length us, event | category | flops | bytes accessed | tf_op | source)
XLA Modules:
  0.0 1531.6 jit_solution(9358067000586807633)
XLA Ops:
  9.7 319.5 %psum.14 = f32[8]{0:T(128)S(1)} all-reduce(f32[8]{0:T(128)S(1)} %reduce_sum.70), channel_id=1, replica_groups=mesh['patch'=128,'chan'=4] {'patch'}, use_global_device_ids=true, to_apply=%region_2.0 | all-reduce | flops 8 | bytes 64 | tf_op jit(solution)/shard_map/psum | solution.py:43
  329.4 0.8 fusion.7
  330.4 309.2 %psum.15 = f32[8]{0:T(128)S(1)} all-reduce(f32[8]{0:T(128)S(1)} %reduce_sum.73), channel_id=1, replica_groups=mesh['patch'=128,'chan'=4] {'patch'}, use_global_device_ids=true, to_apply=%region_5.6 | all-reduce | flops 8 | bytes 64 | tf_op jit(solution)/shard_map/psum | solution.py:46
  640.5 1.2 convolution_reduce_fusion
  641.7 0.8 fusion.14
  642.6 116.3 %all-gather = bf16[4,320,64]{1,2,0:T(8,128)(2,1)S(1)} all-gather(bf16[1,320,64]{1,2,0:T(8,128)(2,1)S(1)} %fusion.14), channel_id=1, replica_groups=mesh['patch'=128,'chan'=4] {'chan'}, dimensions={0}, use_global_device_ids=true | all-gather | bytes 204800 | tf_op jit(solution)/shard_map/all_gather | solution.py:53
  759.2 1.3 convolution_convert_fusion.2
  760.6 1.3 convolution_convert_fusion.1
  762.1 1.3 convolution_convert_fusion
  764.0 12.9 reshape.91
  776.9 528.4 %all-gather.6.cloned.1.call-done = bf16[8192,256]{1,0:T(8,128)(2,1)} async-done(((bf16[64,256]{1,0:T(8,128)(2,1)}), bf16[8192,256]{1,0:T(8,128)(2,1)}) %all-gather.6.cloned.1.call-update) | async-done | bytes 4194320 | tf_op jit(solution)/shard_map/all_gather | solution.py:93
  1305.2 12.9 reshape.92
  1318.1 68.4 %while.14 = (s32[]{:T(128)}, f32[4,64]{1,0:T(4,128)S(1)}, f32[4,64,64]{1,2,0:T(8,128)S(1)}, f32[4,64]{1,0:T(4,128)S(1)}, s32[16]{0:T(128)S(1)}, /*index=5*/s32[]...) while((s32[]{:T(128)}, f32[4,64]{1,0:T(4,128)S(1)}, ...), condition=%wide.region_14.15_spmd, body=%wide.region_8.14_spmd.sunk | while | flops 34890256 | bytes 4054185 | solution.py:110
  1318.2 1.6 constant_dynamic-slice_fusion.3
  1322.4 1.6 constant_dynamic-slice_fusion.3
  1326.7 1.6 constant_dynamic-slice_fusion.3
  1331.0 1.6 constant_dynamic-slice_fusion.3
  1335.3 1.6 constant_dynamic-slice_fusion.3
  1339.5 1.6 constant_dynamic-slice_fusion.3
  1343.8 1.6 constant_dynamic-slice_fusion.3
  1348.1 1.6 constant_dynamic-slice_fusion.3
  1352.4 1.6 constant_dynamic-slice_fusion.3
  1356.6 1.6 constant_dynamic-slice_fusion.3
  1360.9 1.6 constant_dynamic-slice_fusion.3
  1365.2 1.6 constant_dynamic-slice_fusion.3
  1369.5 1.6 constant_dynamic-slice_fusion.3
  1373.8 1.6 constant_dynamic-slice_fusion.3
  1378.0 1.6 constant_dynamic-slice_fusion.3
  1382.3 1.6 constant_dynamic-slice_fusion.3
  1386.9 1.1 copy.67
  1388.0 135.4 %reduce-scatter.4.cloned.1.call-done = f32[320,64]{1,0:T(8,128)} async-done(((f32[1280,64]{1,0:T(8,128)}), f32[320,64]{1,0:T(8,128)}) %reduce-scatter.4.cloned.1.call-update) | async-done | bytes 81936
  1523.4 1.0 copy.68
  (234 shorter events, 37.9 us)
Async XLA Ops:
  7.2 1379.4 %copy-start = (bf16[256,1280]{1,0:T(8,128)(2,1)S(1)}, bf16[256,1280]{1,0:T(8,128)(2,1)}, u32[]{:S(2)}) copy-start(bf16[256,1280]{1,0:T(8,128)(2,1)} %param.21) | copy-start | bytes 1966084
  7.2 756.8 %all-gather.4.cloned.1.call-start = ((), (), s32[]{:S(2)}) async-start(), calls=%async_computation.1 | async-start | bytes 4227072 | tf_op jit(solution)/shard_map/all_gather | solution.py:92
  7.9 1297.3 %all-gather.6.cloned.1.call-start = ((), (), s32[]{:S(2)}) async-start(), calls=%async_computation.2 | async-start | bytes 4227072 | tf_op jit(solution)/shard_map/all_gather | solution.py:93
  8.7 1514.7 %reduce-scatter.4.cloned.1.call-start = ((), (), s32[]{:S(2)}) async-start(), calls=%async_computation.3 | async-start | bytes 819200
  762.0 556.2 %copy-start.2 = (bf16[64,256]{1,0:T(8,128)(2,1)}, bf16[64,256]{1,0:T(8,128)(2,1)S(1)}, u32[]{:S(2)}) copy-start(bf16[64,256]{1,0:T(8,128)(2,1)S(1)} %convolution_convert_fusion.1) | copy-start | bytes 98308
  763.4 554.7 %copy-start.3 = (bf16[64,256]{1,0:T(8,128)(2,1)}, bf16[64,256]{1,0:T(8,128)(2,1)S(1)}, u32[]{:S(2)}) copy-start(bf16[64,256]{1,0:T(8,128)(2,1)S(1)} %convolution_convert_fusion) | copy-start | bytes 98308
  1318.1 206.3 %copy-start.1 = (bf16[64,320]{1,0:T(8,128)(2,1)S(1)}, bf16[64,320]{1,0:T(8,128)(2,1)}, u32[]{:S(2)}) copy-start(bf16[64,320]{1,0:T(8,128)(2,1)} %param.13) | copy-start | bytes 122884
Sparse Core Ops, SparseCore 0:
  10.1 606.6 all-gather.3
  618.9 686.3 all-gather.5
  1388.1 135.2 reduce-scatter.3
where the time goes:
time: 1530 us
  blocking collectives  745 us (49%)
  waiting for transfers between devices  665 us (43%)
  local copies, waits for them, and re-layouts  69.9 us (5%)
  matrix products  15.5 us (1%)
    all_gather x1, waiting for transfers between devices, local(): value_piece = lax.all_gather(stale_values, 'patch', axis=0, tiled=True)  528 us
    psum x1, blocking collectives, local(): group_total = lax.psum(jnp.sum(values, axis=(0, 2)), 'patch')  319 us
    psum x1, blocking collectives, local(): spread = lax.psum(jnp.sum(centered * centered, axis=(0, 2)), 'patch')  309 us
    unnamed x4, waiting for transfers between devices  137 us
    all_gather x1, blocking collectives, local(): shard_piece = lax.all_gather(normed, 'chan', axis=1, tiled=True)  116 us
    dynamic_slice x48, local copies, waits for them, and re-layouts, local(): lax.scan(advance, start_state, (key_steps, value_steps, step_ids))  40.8 us
  transfers between devices with their start and end apart: 3, of which 2 were waited for; matrix products, arithmetic and copies ran while one was open for 1% of the time, Pallas kernels for 0%

commit v1 on v0

--- a/solution.py
+++ b/solution.py
@@ -90,7 +90,9 @@
     )
     start_state = (home_max[..., 0], home_num[:, :, 0], home_den[..., 0])
     key_piece = lax.all_gather(stale_keys, "patch", axis=0, tiled=True)
-    value_piece = lax.all_gather(stale_values, "patch", axis=0, tiled=True)
+    value_piece = jnp.concatenate(
+        lax.all_to_all(jnp.stack([stale_values] * lax.axis_size("patch")), "patch", 0, 0), axis=0
+    )
     slab_count = key_piece.shape[0] // rows_here
     per_step = math.gcd(slab_count, 8)
     key_steps = key_piece.reshape(slab_count // per_step, per_step, rows_here, heads_here, HEAD_DIM)

time: 1530 us -> 1010 us (0.66)
  waiting for transfers between devices: 665 us -> 44.1 us
  blocking collectives: 745 us -> 824 us
  starting transfers between devices: 0.11 us -> 18.4 us
    all_gather x1 -> x0, waiting for transfers between devices: 528 us -> none  [local(): value_piece = lax.all_gather(stale_values, 'patch', axis=0, tiled=True)]
    unnamed x4 -> x3, waiting for transfers between devices: 137 us -> 44.1 us
    psum x1, blocking collectives: 319 us -> 399 us  [local(): group_total = lax.psum(jnp.sum(values, axis=(0, 2)), 'patch')]
    all_to_all x0 -> x1, starting transfers between devices: none -> 18.3 us  [local(): lax.all_to_all(jnp.stack([stale_values] * lax.axis_size('patch')), 'patch...]
    another operation x2 -> x4, local copies, waits for them, and re-layouts: 0.21 us -> 16.5 us  [the longest x1 12.9 us: local(): value_piece.reshape(slab_count // per_step, per_step, rows_here, heads_he...]
  transfers between devices with their start and end apart: 3 -> 3, of which waited for: 2 -> 1; matrix products, arithmetic and copies ran while one was open for 1% -> 2% of each run, Pallas kernels for 0% -> 0%
where the time goes in v1:
time: 1010 us
  blocking collectives  824 us (82%)
  local copies, waits for them, and re-layouts  73.3 us (7%)
  waiting for transfers between devices  44.1 us (4%)
  starting transfers between devices  18.4 us (2%)
  between operations  15 us (1%)
  matrix products  11.2 us (1%)
  loops' own time  10.3 us (1%)
    psum x1, blocking collectives, local(): group_total = lax.psum(jnp.sum(values, axis=(0, 2)), 'patch')  399 us
    psum x1, blocking collectives, local(): spread = lax.psum(jnp.sum(centered * centered, axis=(0, 2)), 'patch')  314 us
    all_gather x1, blocking collectives, local(): shard_piece = lax.all_gather(normed, 'chan', axis=1, tiled=True)  112 us
    unnamed x3, waiting for transfers between devices  44.1 us
    dynamic_slice x48, local copies, waits for them, and re-layouts, local(): lax.scan(advance, start_state, (key_steps, value_steps, step_ids))  40.8 us
  transfers between devices with their start and end apart: 3, of which 1 were waited for; matrix products, arithmetic and copies ran while one was open for 2% of the time, Pallas kernels for 0%

profile of v1, /device:TPU:1, one launch (start us, length us, event | category | flops | bytes accessed | tf_op | source)
XLA Modules:
  0.0 1005.3 jit_solution(5733420351303370536)
XLA Ops:
  7.3 3.4 stack.2
  10.6 18.3 %all-to-all-start = ((bf16[128,64,256]{2,1,0:T(8,128)(2,1)}), bf16[128,64,256]{2,1,0:T(8,128)(2,1)}, u32[]{:S(2)}, u32[]{:S(2)}) async-start(bf16[128,64,256]{2,1,0:T(8,128)(2,1)} %stack.2), calls=%async_computation | async-start | bytes 8388608 | tf_op jit(solution)/shard_map/all_to_all | solution.py:94
  29.0 0.7 all-gather.3.cloned.1.call-update
  30.0 399.0 %psum.14 = f32[8]{0:T(128)S(1)} all-reduce(f32[8]{0:T(128)S(1)} %reduce_sum.70), channel_id=1, replica_groups=mesh['patch'=128,'chan'=4] {'patch'}, use_global_device_ids=true, to_apply=%region_2.0 | all-reduce | flops 8 | bytes 64 | tf_op jit(solution)/shard_map/psum | solution.py:43
  429.4 313.6 %psum.15 = f32[8]{0:T(128)S(1)} all-reduce(f32[8]{0:T(128)S(1)} %reduce_sum.73), channel_id=1, replica_groups=mesh['patch'=128,'chan'=4] {'patch'}, use_global_device_ids=true, to_apply=%region_5.6 | all-reduce | flops 8 | bytes 64 | tf_op jit(solution)/shard_map/psum | solution.py:46
  744.3 111.6 %all-gather = bf16[4,320,64]{1,2,0:T(8,128)(2,1)S(1)} all-gather(bf16[1,320,64]{1,2,0:T(8,128)(2,1)S(1)} %fusion.14), channel_id=1, replica_groups=mesh['patch'=128,'chan'=4] {'chan'}, dimensions={0}, use_global_device_ids=true | all-gather | bytes 204800 | tf_op jit(solution)/shard_map/all_gather | solution.py:53
  857.7 12.9 %reshape_reshape.3 = bf16[16,8,64,4,64]{4,3,2,1,0:T(4,128)(2,1)} reshape(bf16[128,64,256]{2,1,0:T(8,128)(2,1)} %all-to-all-done) | data formatting | bytes 8388608 | tf_op jit(solution)/shard_map/reshape;reshape | solution.py:99
  870.6 12.9 %reshape.89 = bf16[16,8,64,4,64]{4,3,2,1,0:T(4,128)(2,1)} reshape(bf16[8192,256]{1,0:T(8,128)(2,1)} %all-gather.3.cloned.1.call-done) | data formatting | bytes 8388608 | tf_op jit(solution)/shard_map/reshape | solution.py:98
  883.5 68.4 %while.14 = (s32[]{:T(128)}, f32[4,64]{1,0:T(4,128)S(1)}, f32[4,64,64]{1,2,0:T(8,128)S(1)}, f32[4,64]{1,0:T(4,128)S(1)}, s32[16]{0:T(128)S(1)}, /*index=5*/s32[]...) while((s32[]{:T(128)}, f32[4,64]{1,0:T(4,128)S(1)}, ...), condition=%wide.region_14.15_spmd, body=%wide.region_8.14_spmd.sunk | while | flops 34890256 | bytes 4054185 | solution.py:112
  883.5 1.6 constant_dynamic-slice_fusion.3
  887.8 1.6 constant_dynamic-slice_fusion.3
  889.7 0.6 dynamic_slice.16
  892.1 1.6 constant_dynamic-slice_fusion.3
  894.0 0.6 dynamic_slice.16
  896.3 1.6 constant_dynamic-slice_fusion.3
  900.6 1.6 constant_dynamic-slice_fusion.3
  904.9 1.6 constant_dynamic-slice_fusion.3
  906.8 0.6 dynamic_slice.16
  909.2 1.6 constant_dynamic-slice_fusion.3
  913.5 1.6 constant_dynamic-slice_fusion.3
  917.7 1.6 constant_dynamic-slice_fusion.3
  922.0 1.6 constant_dynamic-slice_fusion.3
  926.3 1.6 constant_dynamic-slice_fusion.3
  930.6 1.6 constant_dynamic-slice_fusion.3
  934.8 1.6 constant_dynamic-slice_fusion.3
  939.1 1.6 constant_dynamic-slice_fusion.3
  943.4 1.6 constant_dynamic-slice_fusion.3
  947.7 1.6 constant_dynamic-slice_fusion.3
  952.2 1.1 copy.62
  953.3 43.4 %reduce-scatter.4.cloned.1.call-done = f32[320,64]{1,0:T(8,128)} async-done(((f32[1280,64]{1,0:T(8,128)}), f32[320,64]{1,0:T(8,128)}) %reduce-scatter.4.cloned.1.call-update) | async-done | bytes 81936
  996.8 1.0 copy.63
  997.8 0.6 fusion.12
  (246 shorter events, 34.3 us)
Async XLA Ops:
  7.2 944.8 %copy-start = (bf16[256,1280]{1,0:T(8,128)(2,1)S(1)}, bf16[256,1280]{1,0:T(8,128)(2,1)}, u32[]{:S(2)}) copy-start(bf16[256,1280]{1,0:T(8,128)(2,1)} %param.21) | copy-start | bytes 1966084
  7.2 22.5 %copy-start.1 = (bf16[64,320]{1,0:T(8,128)(2,1)S(1)}, bf16[64,320]{1,0:T(8,128)(2,1)}, u32[]{:S(2)}) copy-start(bf16[64,320]{1,0:T(8,128)(2,1)} %param.13) | copy-start | bytes 122884
  7.2 736.8 %copy-start.5 = (bf16[320,320]{1,0:T(8,128)(2,1)S(1)}, bf16[320,320]{1,0:T(8,128)(2,1)}, u32[]{:S(2)}) copy-start(bf16[320,320]{1,0:T(8,128)(2,1)} %param.17) | copy-start | bytes 614404
  7.2 737.0 %copy-start.9 = (f32[320]{0:T(512)S(1)}, f32[320]{0:T(512)}, u32[]{:S(2)}) copy-start(f32[320]{0:T(512)} %param.15) | copy-start | bytes 3844
  7.2 737.0 %copy-start.8 = (f32[320]{0:T(512)S(1)}, f32[320]{0:T(512)}, u32[]{:S(2)}) copy-start(f32[320]{0:T(512)} %param.16) | copy-start | bytes 3844
  7.2 849.0 %copy-start.2 = (bf16[1280,256]{1,0:T(8,128)(2,1)S(1)}, bf16[1280,256]{1,0:T(8,128)(2,1)}, u32[]{:S(2)}) copy-start(bf16[1280,256]{1,0:T(8,128)(2,1)} %param.18) | copy-start | bytes 1966084
  7.2 849.3 %copy-start.3 = (bf16[1280,256]{1,0:T(8,128)(2,1)S(1)}, bf16[1280,256]{1,0:T(8,128)(2,1)}, u32[]{:S(2)}) copy-start(bf16[1280,256]{1,0:T(8,128)(2,1)} %param.19) | copy-start | bytes 1966084
  7.2 849.7 %copy-start.4 = (bf16[1280,256]{1,0:T(8,128)(2,1)S(1)}, bf16[1280,256]{1,0:T(8,128)(2,1)}, u32[]{:S(2)}) copy-start(bf16[1280,256]{1,0:T(8,128)(2,1)} %param.20) | copy-start | bytes 1966084
  10.6 847.1 %all-to-all-start = ((bf16[128,64,256]{2,1,0:T(8,128)(2,1)}), bf16[128,64,256]{2,1,0:T(8,128)(2,1)}, u32[]{:S(2)}, u32[]{:S(2)}) async-start(bf16[128,64,256]{2,1,0:T(8,128)(2,1)} %stack.2), calls=%async_computation | async-start | bytes 8388608 | tf_op jit(solution)/shard_map/all_to_all | solution.py:94
  28.9 841.7 %all-gather.3.cloned.1.call-start = ((), (), s32[]{:S(2)}) async-start(), calls=%async_computation.2 | async-start | bytes 4227072 | tf_op jit(solution)/shard_map/all_gather | solution.py:92
  29.7 967.1 %reduce-scatter.4.cloned.1.call-start = ((), (), s32[]{:S(2)}) async-start(), calls=%async_computation.3 | async-start | bytes 819200
  856.8 26.7 %copy-start.6 = (bf16[64,256]{1,0:T(8,128)(2,1)}, bf16[64,256]{1,0:T(8,128)(2,1)S(1)}, u32[]{:S(2)}) copy-start(bf16[64,256]{1,0:T(8,128)(2,1)S(1)} %convolution_convert_fusion.1) | copy-start | bytes 98308
  857.2 26.3 %copy-start.7 = (bf16[64,256]{1,0:T(8,128)(2,1)}, bf16[64,256]{1,0:T(8,128)(2,1)S(1)}, u32[]{:S(2)}) copy-start(bf16[64,256]{1,0:T(8,128)(2,1)S(1)} %convolution_convert_fusion) | copy-start | bytes 98308
Sparse Core Ops, SparseCore 0:
  31.8 633.7 all-gather.2
  953.5 43.2 reduce-scatter.3
